TPU v7x, 32 devices: a whole 2x2x4 slice. The times are simulated.
32 devices in a mesh: sub: 8 (over z, x), grp: 4 (over y, core).
Axes of the slice: x: 2, y: 2, z: 4, core: 2. Of those that a mesh axis runs over, the one named last changes fastest.
Arguments:
- resid: float32 [32768, 256], P(('sub', 'grp')), may hold values from -6 to 6
- schur_inv: bfloat16 [65536, 2048], P(('sub', 'grp')), may hold values from -0.125 to 0.125
- basis: bfloat16 [512, 2048], P(('sub', 'grp')), may hold values from -1.5 to 1.5
- scaling: float32 [65536], P(('sub', 'grp')), may hold values from 0.25 to 1
- coarse_inv: bfloat16 [512, 512], P(('sub', 'grp')), may hold values from -0.5 to 0.5
- source_row: int32 [65536], P(('sub', 'grp')), may hold values from 0 to 3071, as said below
- primal_idx: int32 [512], P(('sub', 'grp')), may hold values from 0 to 2047, as said below
Outputs:
- first_apply: float32 [32768, 256], P(('sub', 'grp'))
- second_apply: float32 [32768, 256], P(('sub', 'grp'))
Inputs may be any that keep to these rules, and one draw needn't show every extreme that they name: `source_row`: within one subdomain the entries are distinct; the first subdomain of each chain has none below 1024, the last none at or above 2048. `primal_idx`: within one subdomain the entries are distinct.
All inputs are finite; a program needn't handle non-finite values.
Results may differ from a plain program's by a relative error of at most 0.0076.
Values may be sent and summed in bfloat16 or wider, within the bound.
No kernel may reach another device: no remote copies, remote signals or barrier semaphores. Data moves between devices by JAX's collectives and lax.ppermute only.
A program may use at most 64 MiB of HBM per device.

v0:
```python
import jax
import jax.numpy as jnp
from jax import lax
from jax.sharding import PartitionSpec as P


def with_halo(cells, sides, width):
    for axis, dim in sides:
        count = lax.axis_size(axis)
        ends = count - 1
        head = lax.slice_in_dim(cells, 0, width, axis=dim)
        tail = lax.slice_in_dim(cells, cells.shape[dim] - width, cells.shape[dim], axis=dim)
        cells = jnp.concatenate(
            [
                lax.ppermute(tail, axis, [(i, (i + 1) % count) for i in range(ends)]),
                cells,
                lax.ppermute(head, axis, [((i + 1) % count, i) for i in range(ends)]),
            ],
            axis=dim,
        )
    return cells


def shifted(shard, axis, by):
    devices = lax.axis_size(axis)
    pairs = [(i, i + by) for i in range(devices) if 0 <= i + by < devices]
    return lax.ppermute(shard, axis, pairs)


def shards(resid, schur_inv, basis, scaling, coarse_inv, source_row, primal_idx):
    own_count = resid.shape[0]
    scale_column = scaling[:, None]

    def add_all(portion):
        return jnp.dot(coarse_inv, portion, preferred_element_type=jnp.float32)

    def precondition(vector_in):
        rounded = vector_in.astype(jnp.bfloat16)
        padded = with_halo(rounded, (("sub", 0),), own_count)
        gathered = padded[source_row]
        scaled = (scale_column * gathered.astype(jnp.float32)).astype(jnp.bfloat16)
        primal = scaled[primal_idx]
        coarse = add_all(lax.all_gather(primal, ("sub", "grp"), axis=0, tiled=True))
        coarse_rounded = coarse.astype(jnp.bfloat16)
        solved = jnp.dot(schur_inv, scaled, preferred_element_type=jnp.float32)
        solved = solved + lax.dot_general(
            basis, coarse_rounded, (((0,), (0,)), ((), ())), preferred_element_type=jnp.float32
        )
        weighted = (scale_column * solved).astype(jnp.bfloat16)
        spread = (
            jnp.zeros((3 * own_count, weighted.shape[1]), jnp.bfloat16).at[source_row].set(weighted)
        )
        from_next = shifted(spread[:own_count], "sub", -1)
        from_previous = shifted(spread[2 * own_count :], "sub", 1)
        return (
            spread[own_count : 2 * own_count].astype(jnp.float32)
            + from_next.astype(jnp.float32)
            + from_previous.astype(jnp.float32)
        )

    first_apply = precondition(resid)
    second_apply = precondition(first_apply)
    return (first_apply, second_apply)


def solution(mesh):
    return jax.shard_map(
        shards,
        mesh=mesh,
        in_specs=(
            P(("sub", "grp"), None),
            P(("sub", "grp"), None),
            P(("sub", "grp"), None),
            P(("sub", "grp")),
            P(("sub", "grp"), None),
            P(("sub", "grp")),
            P(("sub", "grp")),
        ),
        out_specs=(P(("sub", "grp"), None), P(("sub", "grp"), None)),
        check_vma=False,
    )
```

profile of v0, /device:TPU:7, one launch (start us, length us, event | category | flops | bytes accessed | tf_op | source)
XLA Modules:
  0.0 236.6 jit_solution(8052517843796168222)
XLA Ops:
  0.6 1.3 convert_element_type.56
  2.0 2.2 collective-permute-start.1
  4.1 4.0 %collective-permute-start = (bf16[1024,256]{1,0:T(8,128)(2,1)S(1)}, bf16[1024,256]{1,0:T(8,128)(2,1)S(1)}, u32[]{:S(2)}, u32[]{:S(2)}) collective-permute-start(bf16[1024,256]{1,0:T(8,128)(2,1)S(1)} %convert_element_type.56), channel_id=1, source_target_pairs={{0,4},{4,8},{8,12},{12,16},{16,20},{20,24},{24,28},{1,5},{5,9},{9,... | collective-permute-start | bytes 1572872 | tf_op jit(solution)/shard_map/ppermute | solution.py:15
  8.2 0.7 compare_select_fusion.1
  8.8 0.7 broadcast_clamp_fusion
  9.5 8.1 %collective-permute-done.1 = bf16[1024,256]{1,0:T(8,128)(2,1)S(1)} collective-permute-done((bf16[1024,256]{1,0:T(8,128)(2,1)S(1)}, bf16[1024,256]{1,0:T(8,128)(2,1)S(1)}, u32[]{:S(2)}, u32[]{:S(2)}) %collective-permute-start.1) | collective-permute-done | bytes 524320 | tf_op jit(solution)/shard_map/ppermute | solution.py:17
  17.6 12.2 %collective-permute-done = bf16[1024,256]{1,0:T(8,128)(2,1)S(1)} collective-permute-done((bf16[1024,256]{1,0:T(8,128)(2,1)S(1)}, bf16[1024,256]{1,0:T(8,128)(2,1)S(1)}, u32[]{:S(2)}, u32[]{:S(2)}) %collective-permute-start) | collective-permute-done | bytes 524320 | tf_op jit(solution)/shard_map/ppermute | solution.py:15
  29.9 7.5 %gather_fusion = bf16[2048,256]{1,0:T(8,128)(2,1)S(1)} fusion(bf16[3072,256]{1,0:T(8,128)(2,1)S(1)} %pad_maximum_fusion, s32[2048]{0:T(1024)S(1)} %get-tuple-element.8), kind=kCustom, calls=%fused_computation | custom fusion | bytes 2105344 | tf_op jit(solution)/shard_map/gather | solution.py:40
  37.8 0.6 gather_fusion.1
  38.4 33.2 %all-gather = bf16[512,256]{1,0:T(8,128)(2,1)S(1)} all-gather(bf16[16,256]{1,0:T(8,128)(2,1)S(1)} %gather_fusion.1), channel_id=2, replica_groups=mesh['sub'=8,'grp'=4] {'sub','grp'}, dimensions={0}, use_global_device_ids=true | all-gather | bytes 270336 | tf_op jit(solution)/shard_map/all_gather | solution.py:43
  71.6 5.8 %fusion.13 = f32[256,2048]{1,0:T(8,128)S(1)} fusion(bf16[2048,256]{1,0:T(8,128)(2,1)S(1)} %multiply_convert_fusion.1, bf16[2048,2048]{1,0:T(8,128)(2,1)} %param.8), kind=kOutput, calls=%fused_computation.33 | convolution fusion | flops 2147483648 | bytes 11534336 | tf_op jit(solution)/shard_map/dot_general | solution.py:45
  77.4 0.7 fusion.5
  78.7 9.8 %scatter_custom_fusion = bf16[3072,256]{1,0:T(8,128)(2,1)S(1)} fusion(s32[2048]{0:T(1024)S(1)} %get-tuple-element.9, bf16[2048,256]{1,0:T(8,128)(2,1)S(1)} %copy.9, bf16[]{:T(256)} %constant.4.clone.1), kind=kCustom, calls=%fused_computation.24 | custom fusion | bytes 1572866 | tf_op jit(solution)/shard_map/scatter | solution.py:51
  88.6 5.8 %collective-permute-start.2 = (bf16[1024,256]{1,0:T(8,128)(2,1)S(1)}, bf16[1024,256]{1,0:T(8,128)(2,1)S(1)}, u32[]{:S(2)}, u32[]{:S(2)}) collective-permute-start(bf16[1024,256]{1,0:T(8,128)(2,1)S(1)} %get-tuple-element.6), channel_id=1, source_target_pairs={{4,0},{8,4},{12,8},{16,12},{20,16},{24,20},{28,24},{5,1},{9,5},{13... | collective-permute-start | bytes 1572872 | tf_op jit(solution)/shard_map/ppermute | solution.py:27
  94.3 1.9 collective-permute-start.3
  96.3 9.2 %collective-permute-done.2 = bf16[1024,256]{1,0:T(8,128)(2,1)S(1)} collective-permute-done((bf16[1024,256]{1,0:T(8,128)(2,1)S(1)}, bf16[1024,256]{1,0:T(8,128)(2,1)S(1)}, u32[]{:S(2)}, u32[]{:S(2)}) %collective-permute-start.2) | collective-permute-done | bytes 524320 | tf_op jit(solution)/shard_map/ppermute | solution.py:27
  105.5 10.9 %collective-permute-done.3 = bf16[1024,256]{1,0:T(8,128)(2,1)S(1)} collective-permute-done((bf16[1024,256]{1,0:T(8,128)(2,1)S(1)}, bf16[1024,256]{1,0:T(8,128)(2,1)S(1)}, u32[]{:S(2)}, u32[]{:S(2)}) %collective-permute-start.3) | collective-permute-done | bytes 524320 | tf_op jit(solution)/shard_map/ppermute | solution.py:27
  116.4 1.2 fusion.10
  117.6 1.9 collective-permute-start.5
  119.5 4.3 %collective-permute-start.4 = (bf16[1024,256]{1,0:T(8,128)(2,1)S(1)}, bf16[1024,256]{1,0:T(8,128)(2,1)S(1)}, u32[]{:S(2)}, u32[]{:S(2)}) collective-permute-start(bf16[1024,256]{1,0:T(8,128)(2,1)S(1)} %get-tuple-element.2), channel_id=1, source_target_pairs={{0,4},{4,8},{8,12},{12,16},{16,20},{20,24},{24,28},{1,5},{5,9},{9,... | collective-permute-start | bytes 1572872 | tf_op jit(solution)/shard_map/ppermute | solution.py:15
  123.8 9.7 %collective-permute-done.5 = bf16[1024,256]{1,0:T(8,128)(2,1)S(1)} collective-permute-done((bf16[1024,256]{1,0:T(8,128)(2,1)S(1)}, bf16[1024,256]{1,0:T(8,128)(2,1)S(1)}, u32[]{:S(2)}, u32[]{:S(2)}) %collective-permute-start.5) | collective-permute-done | bytes 524320 | tf_op jit(solution)/shard_map/ppermute | solution.py:17
  133.4 12.0 %collective-permute-done.4 = bf16[1024,256]{1,0:T(8,128)(2,1)S(1)} collective-permute-done((bf16[1024,256]{1,0:T(8,128)(2,1)S(1)}, bf16[1024,256]{1,0:T(8,128)(2,1)S(1)}, u32[]{:S(2)}, u32[]{:S(2)}) %collective-permute-start.4) | collective-permute-done | bytes 524320 | tf_op jit(solution)/shard_map/ppermute | solution.py:15
  145.6 7.5 %gather_fusion.2 = bf16[2048,256]{1,0:T(8,128)(2,1)S(1)} fusion(bf16[3072,256]{1,0:T(8,128)(2,1)S(1)} %pad_maximum_fusion.1, s32[2048]{0:T(1024)S(1)} %get-tuple-element.8), kind=kCustom, calls=%fused_computation.2 | custom fusion | bytes 2105344 | tf_op jit(solution)/shard_map/gather | solution.py:40
  154.0 5.8 %fusion.14 = f32[256,2048]{1,0:T(8,128)S(1)} fusion(bf16[2048,256]{1,0:T(8,128)(2,1)S(1)} %multiply_convert_fusion, bf16[2048,2048]{1,0:T(8,128)(2,1)} %param.8), kind=kOutput, calls=%fused_computation.34 | convolution fusion | flops 2147483648 | bytes 11534336 | tf_op jit(solution)/shard_map/dot_general | solution.py:45
  159.8 36.6 %all-gather.1 = bf16[512,256]{1,0:T(8,128)(2,1)S(1)} all-gather(bf16[16,256]{1,0:T(8,128)(2,1)S(1)} %gather_fusion.3), channel_id=3, replica_groups=mesh['sub'=8,'grp'=4] {'sub','grp'}, dimensions={0}, use_global_device_ids=true | all-gather | bytes 270336 | tf_op jit(solution)/shard_map/all_gather | solution.py:43
  196.4 0.7 fusion.4
  197.7 9.8 %scatter_custom_fusion.1 = bf16[3072,256]{1,0:T(8,128)(2,1)S(1)} fusion(s32[2048]{0:T(1024)S(1)} %get-tuple-element.9, bf16[2048,256]{1,0:T(8,128)(2,1)S(1)} %copy.10, bf16[]{:T(256)} %constant.4.clone.1), kind=kCustom, calls=%fused_computation.22 | custom fusion | bytes 1572866 | tf_op jit(solution)/shard_map/scatter | solution.py:51
  207.5 5.8 %collective-permute-start.6 = (bf16[1024,256]{1,0:T(8,128)(2,1)S(1)}, bf16[1024,256]{1,0:T(8,128)(2,1)S(1)}, u32[]{:S(2)}, u32[]{:S(2)}) collective-permute-start(bf16[1024,256]{1,0:T(8,128)(2,1)S(1)} %get-tuple-element.4), channel_id=1, source_target_pairs={{4,0},{8,4},{12,8},{16,12},{20,16},{24,20},{28,24},{5,1},{9,5},{13... | collective-permute-start | bytes 1572872 | tf_op jit(solution)/shard_map/ppermute | solution.py:27
  213.3 1.9 collective-permute-start.7
  215.3 9.2 %collective-permute-done.6 = bf16[1024,256]{1,0:T(8,128)(2,1)S(1)} collective-permute-done((bf16[1024,256]{1,0:T(8,128)(2,1)S(1)}, bf16[1024,256]{1,0:T(8,128)(2,1)S(1)}, u32[]{:S(2)}, u32[]{:S(2)}) %collective-permute-start.6) | collective-permute-done | bytes 524320 | tf_op jit(solution)/shard_map/ppermute | solution.py:27
  224.5 10.9 %collective-permute-done.7 = bf16[1024,256]{1,0:T(8,128)(2,1)S(1)} collective-permute-done((bf16[1024,256]{1,0:T(8,128)(2,1)S(1)}, bf16[1024,256]{1,0:T(8,128)(2,1)S(1)}, u32[]{:S(2)}, u32[]{:S(2)}) %collective-permute-start.7) | collective-permute-done | bytes 524320 | tf_op jit(solution)/shard_map/ppermute | solution.py:27
  235.4 1.1 convert_add_fusion
  (16 shorter events, 2.7 us)
Async XLA Ops:
  0.6 76.8 %copy-start = (bf16[16,2048]{1,0:T(8,128)(2,1)S(1)}, bf16[16,2048]{1,0:T(8,128)(2,1)}, u32[]{:S(2)}) copy-start(bf16[16,2048]{1,0:T(8,128)(2,1)} %param.9) | copy-start | bytes 196612
  2.0 15.6 %collective-permute-start.1 = (bf16[1024,256]{1,0:T(8,128)(2,1)S(1)}, bf16[1024,256]{1,0:T(8,128)(2,1)S(1)}, u32[]{:S(2)}, u32[]{:S(2)}) collective-permute-start(bf16[1024,256]{1,0:T(8,128)(2,1)S(1)} %convert_element_type.56), channel_id=1, source_target_pairs={{4,0},{8,4},{12,8},{16,12},{20,16},{24,20},{28,24},{5,1},{9,5},{13... | collective-permute-start | bytes 1572872 | tf_op jit(solution)/shard_map/ppermute | solution.py:17
  4.1 25.7 %collective-permute-start = (bf16[1024,256]{1,0:T(8,128)(2,1)S(1)}, bf16[1024,256]{1,0:T(8,128)(2,1)S(1)}, u32[]{:S(2)}, u32[]{:S(2)}) collective-permute-start(bf16[1024,256]{1,0:T(8,128)(2,1)S(1)} %convert_element_type.56), channel_id=1, source_target_pairs={{0,4},{4,8},{8,12},{12,16},{16,20},{20,24},{24,28},{1,5},{5,9},{9,... | collective-permute-start | bytes 1572872 | tf_op jit(solution)/shard_map/ppermute | solution.py:15
  29.9 7.5 %copy-start.1 = (f32[2048]{0:T(1024)S(1)}, f32[2048]{0:T(1024)}, u32[]{:S(2)}) copy-start(f32[2048]{0:T(1024)} %param.10) | copy-start | bytes 24580
  71.6 5.8 %copy-start.2 = (bf16[16,512]{1,0:T(8,128)(2,1)S(1)}, bf16[16,512]{1,0:T(8,128)(2,1)}, u32[]{:S(2)}) copy-start(bf16[16,512]{1,0:T(8,128)(2,1)} %param.11) | copy-start | bytes 49156
  88.6 16.9 %collective-permute-start.2 = (bf16[1024,256]{1,0:T(8,128)(2,1)S(1)}, bf16[1024,256]{1,0:T(8,128)(2,1)S(1)}, u32[]{:S(2)}, u32[]{:S(2)}) collective-permute-start(bf16[1024,256]{1,0:T(8,128)(2,1)S(1)} %get-tuple-element.6), channel_id=1, source_target_pairs={{4,0},{8,4},{12,8},{16,12},{20,16},{24,20},{28,24},{5,1},{9,5},{13... | collective-permute-start | bytes 1572872 | tf_op jit(solution)/shard_map/ppermute | solution.py:27
  94.3 22.1 %collective-permute-start.3 = (bf16[1024,256]{1,0:T(8,128)(2,1)S(1)}, bf16[1024,256]{1,0:T(8,128)(2,1)S(1)}, u32[]{:S(2)}, u32[]{:S(2)}) collective-permute-start(bf16[1024,256]{1,0:T(8,128)(2,1)S(1)} %get-tuple-element.7), channel_id=1, source_target_pairs={{0,4},{4,8},{8,12},{12,16},{16,20},{20,24},{24,28},{1,5},{5,9},{9,... | collective-permute-start | bytes 1572872 | tf_op jit(solution)/shard_map/ppermute | solution.py:27
  117.6 15.8 %collective-permute-start.5 = (bf16[1024,256]{1,0:T(8,128)(2,1)S(1)}, bf16[1024,256]{1,0:T(8,128)(2,1)S(1)}, u32[]{:S(2)}, u32[]{:S(2)}) collective-permute-start(bf16[1024,256]{1,0:T(8,128)(2,1)S(1)} %get-tuple-element.2), channel_id=1, source_target_pairs={{4,0},{8,4},{12,8},{16,12},{20,16},{24,20},{28,24},{5,1},{9,5},{13... | collective-permute-start | bytes 1572872 | tf_op jit(solution)/shard_map/ppermute | solution.py:17
  119.5 25.9 %collective-permute-start.4 = (bf16[1024,256]{1,0:T(8,128)(2,1)S(1)}, bf16[1024,256]{1,0:T(8,128)(2,1)S(1)}, u32[]{:S(2)}, u32[]{:S(2)}) collective-permute-start(bf16[1024,256]{1,0:T(8,128)(2,1)S(1)} %get-tuple-element.2), channel_id=1, source_target_pairs={{0,4},{4,8},{8,12},{12,16},{16,20},{20,24},{24,28},{1,5},{5,9},{9,... | collective-permute-start | bytes 1572872 | tf_op jit(solution)/shard_map/ppermute | solution.py:15
  207.5 16.9 %collective-permute-start.6 = (bf16[1024,256]{1,0:T(8,128)(2,1)S(1)}, bf16[1024,256]{1,0:T(8,128)(2,1)S(1)}, u32[]{:S(2)}, u32[]{:S(2)}) collective-permute-start(bf16[1024,256]{1,0:T(8,128)(2,1)S(1)} %get-tuple-element.4), channel_id=1, source_target_pairs={{4,0},{8,4},{12,8},{16,12},{20,16},{24,20},{28,24},{5,1},{9,5},{13... | collective-permute-start | bytes 1572872 | tf_op jit(solution)/shard_map/ppermute | solution.py:27
  213.3 22.1 %collective-permute-start.7 = (bf16[1024,256]{1,0:T(8,128)(2,1)S(1)}, bf16[1024,256]{1,0:T(8,128)(2,1)S(1)}, u32[]{:S(2)}, u32[]{:S(2)}) collective-permute-start(bf16[1024,256]{1,0:T(8,128)(2,1)S(1)} %get-tuple-element.5), channel_id=1, source_target_pairs={{0,4},{4,8},{8,12},{12,16},{16,20},{20,24},{24,28},{1,5},{5,9},{9,... | collective-permute-start | bytes 1572872 | tf_op jit(solution)/shard_map/ppermute | solution.py:27
where the time goes:
time: 237 us
  waiting for transfers between devices  82.3 us (35%)
  blocking collectives  69.9 us (29%)
  local copies, waits for them, and re-layouts  36.9 us (16%)
  starting transfers between devices  27.8 us (12%)
  matrix products  13 us (5%)
  other arithmetic  5.86 us (2%)
    all_gather x2, blocking collectives, precondition(): coarse = add_all(lax.all_gather(primal, ('sub', 'grp'), axis=0, tiled=True))  69.9 us
    ppermute x4, waiting for transfers between devices, shifted(): return lax.ppermute(shard, axis, pairs)  40.3 us
    ppermute x2, waiting for transfers between devices, with_halo(): lax.ppermute(tail, axis, [(i, (i + 1) % count) for i in range(ends)])  24.3 us
    scatter x2, local copies, waits for them, and re-layouts, precondition(): jnp.zeros((3 * own_count, weighted.shape[1]), jnp.bfloat16).at[source_row]  19.6 us
    ppermute x2, waiting for transfers between devices, with_halo(): lax.ppermute(head, axis, [((i + 1) % count, i) for i in range(ends)])  17.7 us
    ppermute x4, starting transfers between devices, shifted(): return lax.ppermute(shard, axis, pairs)  15.4 us
    gather x2, local copies, waits for them, and re-layouts, precondition(): gathered = padded[source_row]  15 us
    dot_general x2, matrix products, precondition(): solved = jnp.dot(schur_inv, scaled, preferred_element_type=jnp.float32)  11.5 us
  transfers between devices with their start and end apart: 8, of which 8 were waited for; matrix products, arithmetic and copies ran while one was open for 1% of the time, Pallas kernels for 0%

commit v1 on v0

--- a/solution.py
+++ b/solution.py
@@ -2,6 +2,18 @@
 import jax.numpy as jnp
 from jax import lax
 from jax.sharding import PartitionSpec as P
+
+
+def doubled_up(x, axis, dim):
+    ways, here, step = (lax.axis_size(axis), lax.axis_index(axis), x.shape[dim])
+    line, have = (x, 1)
+    while have < ways:
+        line = jnp.concatenate(
+            [line, lax.ppermute(line, axis, [(d, (d - have) % ways) for d in range(ways)])],
+            axis=dim,
+        )
+        have = 2 * have
+    return jnp.roll(line, here * step, axis=dim)
 
 
 def with_halo(cells, sides, width):
@@ -40,7 +52,7 @@
         gathered = padded[source_row]
         scaled = (scale_column * gathered.astype(jnp.float32)).astype(jnp.bfloat16)
         primal = scaled[primal_idx]
-        coarse = add_all(lax.all_gather(primal, ("sub", "grp"), axis=0, tiled=True))
+        coarse = add_all(doubled_up(primal, ("sub", "grp"), 0))
         coarse_rounded = coarse.astype(jnp.bfloat16)
         solved = jnp.dot(schur_inv, scaled, preferred_element_type=jnp.float32)
         solved = solved + lax.dot_general(

time: 237 us -> 210 us (0.89)
  blocking collectives: 69.9 us -> 0 us
  waiting for transfers between devices: 82.3 us -> 120 us
  starting transfers between devices: 27.8 us -> 32 us
    all_gather x2 -> x0, blocking collectives: 69.9 us -> none  [precondition(): coarse = add_all(lax.all_gather(primal, ('sub', 'grp'), axis=0, tiled=True))]
    ppermute x0 -> x10, waiting for transfers between devices: none -> 34.6 us  [doubled_up(): lax.ppermute(line, axis, [(d, (d - have) % ways) for d in range(ways)])]
    ppermute x0 -> x10, starting transfers between devices: none -> 7.32 us  [doubled_up(): lax.ppermute(line, axis, [(d, (d - have) % ways) for d in range(ways)])]
    ppermute x4, starting transfers between devices: 15.4 us -> 12.4 us  [shifted(): return lax.ppermute(shard, axis, pairs)]
    ppermute x4, waiting for transfers between devices: 40.3 us -> 43.4 us  [shifted(): return lax.ppermute(shard, axis, pairs)]
  transfers between devices with their start and end apart: 8 -> 18, of which waited for: 8 -> 18; matrix products, arithmetic and copies ran while one was open for 1% -> 6% of each run, Pallas kernels for 0% -> 0%
where the time goes in v1:
time: 210 us
  waiting for transfers between devices  120 us (57%)
  local copies, waits for them, and re-layouts  37 us (18%)
  starting transfers between devices  32 us (15%)
  matrix products  13.8 us (7%)
  other arithmetic  5.88 us (3%)
    ppermute x4, waiting for transfers between devices, shifted(): return lax.ppermute(shard, axis, pairs)  43.4 us
    ppermute x10, waiting for transfers between devices, doubled_up(): lax.ppermute(line, axis, [(d, (d - have) % ways) for d in range(ways)])  34.6 us
    ppermute x2, waiting for transfers between devices, with_halo(): lax.ppermute(tail, axis, [(i, (i + 1) % count) for i in range(ends)])  24.3 us
    scatter x2, local copies, waits for them, and re-layouts, precondition(): jnp.zeros((3 * own_count, weighted.shape[1]), jnp.bfloat16).at[source_row]  19.6 us
    ppermute x2, waiting for transfers between devices, with_halo(): lax.ppermute(head, axis, [((i + 1) % count, i) for i in range(ends)])  17.7 us
    gather x2, local copies, waits for them, and re-layouts, precondition(): gathered = padded[source_row]  15 us
    ppermute x4, starting transfers between devices, shifted(): return lax.ppermute(shard, axis, pairs)  12.4 us
    dot_general x2, matrix products, precondition(): solved = jnp.dot(schur_inv, scaled, preferred_element_type=jnp.float32)  11.5 us
  transfers between devices with their start and end apart: 18, of which 18 were waited for; matrix products, arithmetic and copies ran while one was open for 6% of the time, Pallas kernels for 0%

profile of v1, /device:TPU:7, one launch (start us, length us, event | category | flops | bytes accessed | tf_op | source)
XLA Modules:
  0.0 209.6 jit_solution(1834717620619819092)
XLA Ops:
  2.0 2.2 %collective-permute-start.1 = (bf16[1024,256]{1,0:T(8,128)(2,1)S(1)}, bf16[1024,256]{1,0:T(8,128)(2,1)S(1)}, u32[]{:S(2)}, u32[]{:S(2)}) collective-permute-start(bf16[1024,256]{1,0:T(8,128)(2,1)S(1)} %convert_element_type.56), channel_id=1, source_target_pairs={{4,0},{8,4},{12,8},{16,12},{20,16},{24,20},{28,24},{5,1},{9,5},{13... | collective-permute-start | bytes 1572872 | tf_op jit(solution)/shard_map/ppermute | solution.py:29
  4.1 4.0 %collective-permute-start = (bf16[1024,256]{1,0:T(8,128)(2,1)S(1)}, bf16[1024,256]{1,0:T(8,128)(2,1)S(1)}, u32[]{:S(2)}, u32[]{:S(2)}) collective-permute-start(bf16[1024,256]{1,0:T(8,128)(2,1)S(1)} %convert_element_type.56), channel_id=1, source_target_pairs={{0,4},{4,8},{8,12},{12,16},{16,20},{20,24},{24,28},{1,5},{5,9},{9,... | collective-permute-start | bytes 1572872 | tf_op jit(solution)/shard_map/ppermute | solution.py:27
  9.5 8.0 %collective-permute-done.1 = bf16[1024,256]{1,0:T(8,128)(2,1)S(1)} collective-permute-done((bf16[1024,256]{1,0:T(8,128)(2,1)S(1)}, bf16[1024,256]{1,0:T(8,128)(2,1)S(1)}, u32[]{:S(2)}, u32[]{:S(2)}) %collective-permute-start.1) | collective-permute-done | bytes 524320 | tf_op jit(solution)/shard_map/ppermute | solution.py:29
  17.6 12.2 %collective-permute-done = bf16[1024,256]{1,0:T(8,128)(2,1)S(1)} collective-permute-done((bf16[1024,256]{1,0:T(8,128)(2,1)S(1)}, bf16[1024,256]{1,0:T(8,128)(2,1)S(1)}, u32[]{:S(2)}, u32[]{:S(2)}) %collective-permute-start) | collective-permute-done | bytes 524320 | tf_op jit(solution)/shard_map/ppermute | solution.py:27
  29.9 7.5 %gather_fusion = bf16[2048,256]{1,0:T(8,128)(2,1)S(1)} fusion(bf16[3072,256]{1,0:T(8,128)(2,1)S(1)} %pad_maximum_fusion, s32[2048]{0:T(1024)S(1)} %get-tuple-element.29), kind=kCustom, calls=%fused_computation | custom fusion | bytes 2105344 | tf_op jit(solution)/shard_map/gather | solution.py:52
  39.0 4.4 %collective-permute-done.2 = bf16[16,256]{1,0:T(8,128)(2,1)S(1)} collective-permute-done((bf16[16,256]{1,0:T(8,128)(2,1)S(1)}, bf16[16,256]{1,0:T(8,128)(2,1)S(1)}, u32[]{:S(2)}, u32[]{:S(2)}) %collective-permute-start.2) | collective-permute-done | bytes 8224 | tf_op jit(solution)/shard_map/ppermute | solution.py:12
  43.3 4.4 %collective-permute-done.3 = bf16[32,256]{1,0:T(8,128)(2,1)S(1)} collective-permute-done((bf16[32,256]{1,0:T(8,128)(2,1)S(1)}, bf16[32,256]{1,0:T(8,128)(2,1)S(1)}, u32[]{:S(2)}, u32[]{:S(2)}) %collective-permute-start.3) | collective-permute-done | bytes 16416 | tf_op jit(solution)/shard_map/ppermute | solution.py:12
  47.7 3.7 %collective-permute-done.4 = bf16[64,256]{1,0:T(8,128)(2,1)S(1)} collective-permute-done((bf16[64,256]{1,0:T(8,128)(2,1)S(1)}, bf16[64,256]{1,0:T(8,128)(2,1)S(1)}, u32[]{:S(2)}, u32[]{:S(2)}) %collective-permute-start.4) | collective-permute-done | bytes 32800 | tf_op jit(solution)/shard_map/ppermute | solution.py:12
  51.4 4.8 %collective-permute-start.5 = (bf16[128,256]{1,0:T(8,128)(2,1)S(1)}, bf16[128,256]{1,0:T(8,128)(2,1)S(1)}, u32[]{:S(2)}, u32[]{:S(2)}) collective-permute-start(bf16[128,256]{1,0:T(8,128)(2,1)S(1)} %pad_maximum_fusion.2), channel_id=1, source_target_pairs={{0,24},{1,25},{2,26},{3,27},{4,28},{5,29},{6,30},{7,31},{8,0},{9,1... | collective-permute-start | bytes 196616 | tf_op jit(solution)/shard_map/ppermute | solution.py:12
  58.2 5.8 %fusion.27 = f32[256,2048]{1,0:T(8,128)S(1)} fusion(bf16[2048,256]{1,0:T(8,128)(2,1)S(1)} %multiply_convert_fusion.1, bf16[2048,2048]{1,0:T(8,128)(2,1)} %param.10), kind=kOutput, calls=%fused_computation.71 | convolution fusion | flops 2147483648 | bytes 11534336 | tf_op jit(solution)/shard_map/dot_general | solution.py:57
  64.0 2.6 %collective-permute-done.6 = bf16[256,256]{1,0:T(8,128)(2,1)S(1)} collective-permute-done((bf16[256,256]{1,0:T(8,128)(2,1)S(1)}, bf16[256,256]{1,0:T(8,128)(2,1)S(1)}, u32[]{:S(2)}, u32[]{:S(2)}) %collective-permute-start.6) | collective-permute-done | bytes 131104 | tf_op jit(solution)/shard_map/ppermute | solution.py:12
  68.3 9.8 %scatter_custom_fusion = bf16[3072,256]{1,0:T(8,128)(2,1)S(1)} fusion(s32[2048]{0:T(1024)S(1)} %get-tuple-element.30, bf16[2048,256]{1,0:T(8,128)(2,1)S(1)} %copy.9, bf16[]{:T(256)} %constant.30.clone.1), kind=kCustom, calls=%fused_computation.24 | custom fusion | bytes 1572866 | tf_op jit(solution)/shard_map/scatter | solution.py:63
  78.2 1.9 collective-permute-start.7
  80.1 4.3 %collective-permute-start.8 = (bf16[1024,256]{1,0:T(8,128)(2,1)S(1)}, bf16[1024,256]{1,0:T(8,128)(2,1)S(1)}, u32[]{:S(2)}, u32[]{:S(2)}) collective-permute-start(bf16[1024,256]{1,0:T(8,128)(2,1)S(1)} %get-tuple-element.8), channel_id=1, source_target_pairs={{0,4},{4,8},{8,12},{12,16},{16,20},{20,24},{24,28},{1,5},{5,9},{9,... | collective-permute-start | bytes 1572872 | tf_op jit(solution)/shard_map/ppermute | solution.py:39
  84.4 9.7 %collective-permute-done.7 = bf16[1024,256]{1,0:T(8,128)(2,1)S(1)} collective-permute-done((bf16[1024,256]{1,0:T(8,128)(2,1)S(1)}, bf16[1024,256]{1,0:T(8,128)(2,1)S(1)}, u32[]{:S(2)}, u32[]{:S(2)}) %collective-permute-start.7) | collective-permute-done | bytes 524320 | tf_op jit(solution)/shard_map/ppermute | solution.py:39
  94.1 11.9 %collective-permute-done.8 = bf16[1024,256]{1,0:T(8,128)(2,1)S(1)} collective-permute-done((bf16[1024,256]{1,0:T(8,128)(2,1)S(1)}, bf16[1024,256]{1,0:T(8,128)(2,1)S(1)}, u32[]{:S(2)}, u32[]{:S(2)}) %collective-permute-start.8) | collective-permute-done | bytes 524320 | tf_op jit(solution)/shard_map/ppermute | solution.py:39
  107.2 1.9 collective-permute-start.10
  109.1 4.3 %collective-permute-start.9 = (bf16[1024,256]{1,0:T(8,128)(2,1)S(1)}, bf16[1024,256]{1,0:T(8,128)(2,1)S(1)}, u32[]{:S(2)}, u32[]{:S(2)}) collective-permute-start(bf16[1024,256]{1,0:T(8,128)(2,1)S(1)} %get-tuple-element.3), channel_id=1, source_target_pairs={{0,4},{4,8},{8,12},{12,16},{16,20},{20,24},{24,28},{1,5},{5,9},{9,... | collective-permute-start | bytes 1572872 | tf_op jit(solution)/shard_map/ppermute | solution.py:27
  113.4 9.7 %collective-permute-done.10 = bf16[1024,256]{1,0:T(8,128)(2,1)S(1)} collective-permute-done((bf16[1024,256]{1,0:T(8,128)(2,1)S(1)}, bf16[1024,256]{1,0:T(8,128)(2,1)S(1)}, u32[]{:S(2)}, u32[]{:S(2)}) %collective-permute-start.10) | collective-permute-done | bytes 524320 | tf_op jit(solution)/shard_map/ppermute | solution.py:29
  123.0 12.0 %collective-permute-done.9 = bf16[1024,256]{1,0:T(8,128)(2,1)S(1)} collective-permute-done((bf16[1024,256]{1,0:T(8,128)(2,1)S(1)}, bf16[1024,256]{1,0:T(8,128)(2,1)S(1)}, u32[]{:S(2)}, u32[]{:S(2)}) %collective-permute-start.9) | collective-permute-done | bytes 524320 | tf_op jit(solution)/shard_map/ppermute | solution.py:27
  135.2 7.5 %gather_fusion.2 = bf16[2048,256]{1,0:T(8,128)(2,1)S(1)} fusion(bf16[3072,256]{1,0:T(8,128)(2,1)S(1)} %pad_maximum_fusion.1, s32[2048]{0:T(1024)S(1)} %get-tuple-element.29), kind=kCustom, calls=%fused_computation.2 | custom fusion | bytes 2105344 | tf_op jit(solution)/shard_map/gather | solution.py:52
  144.2 4.4 %collective-permute-done.11 = bf16[16,256]{1,0:T(8,128)(2,1)S(1)} collective-permute-done((bf16[16,256]{1,0:T(8,128)(2,1)S(1)}, bf16[16,256]{1,0:T(8,128)(2,1)S(1)}, u32[]{:S(2)}, u32[]{:S(2)}) %collective-permute-start.11) | collective-permute-done | bytes 8224 | tf_op jit(solution)/shard_map/ppermute | solution.py:12
  148.6 4.4 %collective-permute-done.12 = bf16[32,256]{1,0:T(8,128)(2,1)S(1)} collective-permute-done((bf16[32,256]{1,0:T(8,128)(2,1)S(1)}, bf16[32,256]{1,0:T(8,128)(2,1)S(1)}, u32[]{:S(2)}, u32[]{:S(2)}) %collective-permute-start.12) | collective-permute-done | bytes 16416 | tf_op jit(solution)/shard_map/ppermute | solution.py:12
  153.0 3.7 %collective-permute-done.13 = bf16[64,256]{1,0:T(8,128)(2,1)S(1)} collective-permute-done((bf16[64,256]{1,0:T(8,128)(2,1)S(1)}, bf16[64,256]{1,0:T(8,128)(2,1)S(1)}, u32[]{:S(2)}, u32[]{:S(2)}) %collective-permute-start.13) | collective-permute-done | bytes 32800 | tf_op jit(solution)/shard_map/ppermute | solution.py:12
  157.3 2.9 %collective-permute-done.14 = bf16[128,256]{1,0:T(8,128)(2,1)S(1)} collective-permute-done((bf16[128,256]{1,0:T(8,128)(2,1)S(1)}, bf16[128,256]{1,0:T(8,128)(2,1)S(1)}, u32[]{:S(2)}, u32[]{:S(2)}) %collective-permute-start.14) | collective-permute-done | bytes 65568 | tf_op jit(solution)/shard_map/ppermute | solution.py:12
  160.3 5.8 %fusion.28 = f32[256,2048]{1,0:T(8,128)S(1)} fusion(bf16[2048,256]{1,0:T(8,128)(2,1)S(1)} %multiply_convert_fusion, bf16[2048,2048]{1,0:T(8,128)(2,1)} %param.10), kind=kOutput, calls=%fused_computation.72 | convolution fusion | flops 2147483648 | bytes 11534336 | tf_op jit(solution)/shard_map/dot_general | solution.py:57
  166.1 2.9 %collective-permute-done.15 = bf16[256,256]{1,0:T(8,128)(2,1)S(1)} collective-permute-done((bf16[256,256]{1,0:T(8,128)(2,1)S(1)}, bf16[256,256]{1,0:T(8,128)(2,1)S(1)}, u32[]{:S(2)}, u32[]{:S(2)}) %collective-permute-start.15) | collective-permute-done | bytes 131104 | tf_op jit(solution)/shard_map/ppermute | solution.py:12
  170.7 9.8 %scatter_custom_fusion.1 = bf16[3072,256]{1,0:T(8,128)(2,1)S(1)} fusion(s32[2048]{0:T(1024)S(1)} %get-tuple-element.30, bf16[2048,256]{1,0:T(8,128)(2,1)S(1)} %copy.10, bf16[]{:T(256)} %constant.30.clone.1), kind=kCustom, calls=%fused_computation.22 | custom fusion | bytes 1572866 | tf_op jit(solution)/shard_map/scatter | solution.py:63
  180.6 1.9 collective-permute-start.16
  182.5 4.3 %collective-permute-start.17 = (bf16[1024,256]{1,0:T(8,128)(2,1)S(1)}, bf16[1024,256]{1,0:T(8,128)(2,1)S(1)}, u32[]{:S(2)}, u32[]{:S(2)}) collective-permute-start(bf16[1024,256]{1,0:T(8,128)(2,1)S(1)} %get-tuple-element.6), channel_id=1, source_target_pairs={{0,4},{4,8},{8,12},{12,16},{16,20},{20,24},{24,28},{1,5},{5,9},{9,... | collective-permute-start | bytes 1572872 | tf_op jit(solution)/shard_map/ppermute | solution.py:39
  186.8 9.2 %collective-permute-done.16 = bf16[1024,256]{1,0:T(8,128)(2,1)S(1)} collective-permute-done((bf16[1024,256]{1,0:T(8,128)(2,1)S(1)}, bf16[1024,256]{1,0:T(8,128)(2,1)S(1)}, u32[]{:S(2)}, u32[]{:S(2)}) %collective-permute-start.16) | collective-permute-done | bytes 524320 | tf_op jit(solution)/shard_map/ppermute | solution.py:39
  195.9 12.5 %collective-permute-done.17 = bf16[1024,256]{1,0:T(8,128)(2,1)S(1)} collective-permute-done((bf16[1024,256]{1,0:T(8,128)(2,1)S(1)}, bf16[1024,256]{1,0:T(8,128)(2,1)S(1)}, u32[]{:S(2)}, u32[]{:S(2)}) %collective-permute-start.17) | collective-permute-done | bytes 524320 | tf_op jit(solution)/shard_map/ppermute | solution.py:39
  (52 shorter events, 14.4 us)
Async XLA Ops:
  0.6 66.0 %copy-start = (bf16[16,2048]{1,0:T(8,128)(2,1)S(1)}, bf16[16,2048]{1,0:T(8,128)(2,1)}, u32[]{:S(2)}) copy-start(bf16[16,2048]{1,0:T(8,128)(2,1)} %param.11) | copy-start | bytes 196612
  2.0 15.6 %collective-permute-start.1 = (bf16[1024,256]{1,0:T(8,128)(2,1)S(1)}, bf16[1024,256]{1,0:T(8,128)(2,1)S(1)}, u32[]{:S(2)}, u32[]{:S(2)}) collective-permute-start(bf16[1024,256]{1,0:T(8,128)(2,1)S(1)} %convert_element_type.56), channel_id=1, source_target_pairs={{4,0},{8,4},{12,8},{16,12},{20,16},{24,20},{28,24},{5,1},{9,5},{13... | collective-permute-start | bytes 1572872 | tf_op jit(solution)/shard_map/ppermute | solution.py:29
  4.1 25.7 %collective-permute-start = (bf16[1024,256]{1,0:T(8,128)(2,1)S(1)}, bf16[1024,256]{1,0:T(8,128)(2,1)S(1)}, u32[]{:S(2)}, u32[]{:S(2)}) collective-permute-start(bf16[1024,256]{1,0:T(8,128)(2,1)S(1)} %convert_element_type.56), channel_id=1, source_target_pairs={{0,4},{4,8},{8,12},{12,16},{16,20},{20,24},{24,28},{1,5},{5,9},{9,... | collective-permute-start | bytes 1572872 | tf_op jit(solution)/shard_map/ppermute | solution.py:27
  29.9 7.5 %copy-start.1 = (f32[2048]{0:T(1024)S(1)}, f32[2048]{0:T(1024)}, u32[]{:S(2)}) copy-start(f32[2048]{0:T(1024)} %param.12) | copy-start | bytes 24580
  38.4 4.9 %collective-permute-start.2 = (bf16[16,256]{1,0:T(8,128)(2,1)S(1)}, bf16[16,256]{1,0:T(8,128)(2,1)S(1)}, u32[]{:S(2)}, u32[]{:S(2)}) collective-permute-start(bf16[16,256]{1,0:T(8,128)(2,1)S(1)} %gather_fusion.1), channel_id=1, source_target_pairs={{0,31},{1,0},{2,1},{3,2},{4,3},{5,4},{6,5},{7,6},{8,7},{9,8},{10,9... | collective-permute-start | bytes 24584 | tf_op jit(solution)/shard_map/ppermute | solution.py:12
  43.3 4.4 %collective-permute-start.3 = (bf16[32,256]{1,0:T(8,128)(2,1)S(1)}, bf16[32,256]{1,0:T(8,128)(2,1)S(1)}, u32[]{:S(2)}, u32[]{:S(2)}) collective-permute-start(bf16[32,256]{1,0:T(8,128)(2,1)S(1)} %pad_maximum_fusion.6), channel_id=1, source_target_pairs={{0,30},{1,31},{2,0},{3,1},{4,2},{5,3},{6,4},{7,5},{8,6},{9,7},{10,... | collective-permute-start | bytes 49160 | tf_op jit(solution)/shard_map/ppermute | solution.py:12
  47.7 3.7 %collective-permute-start.4 = (bf16[64,256]{1,0:T(8,128)(2,1)S(1)}, bf16[64,256]{1,0:T(8,128)(2,1)S(1)}, u32[]{:S(2)}, u32[]{:S(2)}) collective-permute-start(bf16[64,256]{1,0:T(8,128)(2,1)S(1)} %pad_maximum_fusion.4), channel_id=1, source_target_pairs={{0,28},{1,29},{2,30},{3,31},{4,0},{5,1},{6,2},{7,3},{8,4},{9,5},{1... | collective-permute-start | bytes 98312 | tf_op jit(solution)/shard_map/ppermute | solution.py:12
  51.4 6.2 %collective-permute-start.5 = (bf16[128,256]{1,0:T(8,128)(2,1)S(1)}, bf16[128,256]{1,0:T(8,128)(2,1)S(1)}, u32[]{:S(2)}, u32[]{:S(2)}) collective-permute-start(bf16[128,256]{1,0:T(8,128)(2,1)S(1)} %pad_maximum_fusion.2), channel_id=1, source_target_pairs={{0,24},{1,25},{2,26},{3,27},{4,28},{5,29},{6,30},{7,31},{8,0},{9,1... | collective-permute-start | bytes 196616 | tf_op jit(solution)/shard_map/ppermute | solution.py:12
  57.6 9.0 %copy-start.2 = (bf16[16,512]{1,0:T(8,128)(2,1)S(1)}, bf16[16,512]{1,0:T(8,128)(2,1)}, u32[]{:S(2)}) copy-start(bf16[16,512]{1,0:T(8,128)(2,1)} %param.13) | copy-start | bytes 49156
  57.6 9.0 %collective-permute-start.6 = (bf16[256,256]{1,0:T(8,128)(2,1)S(1)}, bf16[256,256]{1,0:T(8,128)(2,1)S(1)}, u32[]{:S(2)}, u32[]{:S(2)}) collective-permute-start(bf16[256,256]{1,0:T(8,128)(2,1)S(1)} %get-tuple-element.11), channel_id=1, source_target_pairs={{0,16},{1,17},{2,18},{3,19},{4,20},{5,21},{6,22},{7,23},{8,24},{9,... | collective-permute-start | bytes 393224 | tf_op jit(solution)/shard_map/ppermute | solution.py:12
  78.2 15.9 %collective-permute-start.7 = (bf16[1024,256]{1,0:T(8,128)(2,1)S(1)}, bf16[1024,256]{1,0:T(8,128)(2,1)S(1)}, u32[]{:S(2)}, u32[]{:S(2)}) collective-permute-start(bf16[1024,256]{1,0:T(8,128)(2,1)S(1)} %get-tuple-element.7), channel_id=1, source_target_pairs={{4,0},{8,4},{12,8},{16,12},{20,16},{24,20},{28,24},{5,1},{9,5},{13... | collective-permute-start | bytes 1572872 | tf_op jit(solution)/shard_map/ppermute | solution.py:39
  80.1 26.0 %collective-permute-start.8 = (bf16[1024,256]{1,0:T(8,128)(2,1)S(1)}, bf16[1024,256]{1,0:T(8,128)(2,1)S(1)}, u32[]{:S(2)}, u32[]{:S(2)}) collective-permute-start(bf16[1024,256]{1,0:T(8,128)(2,1)S(1)} %get-tuple-element.8), channel_id=1, source_target_pairs={{0,4},{4,8},{8,12},{12,16},{16,20},{20,24},{24,28},{1,5},{5,9},{9,... | collective-permute-start | bytes 1572872 | tf_op jit(solution)/shard_map/ppermute | solution.py:39
  107.2 15.8 %collective-permute-start.10 = (bf16[1024,256]{1,0:T(8,128)(2,1)S(1)}, bf16[1024,256]{1,0:T(8,128)(2,1)S(1)}, u32[]{:S(2)}, u32[]{:S(2)}) collective-permute-start(bf16[1024,256]{1,0:T(8,128)(2,1)S(1)} %get-tuple-element.3), channel_id=1, source_target_pairs={{4,0},{8,4},{12,8},{16,12},{20,16},{24,20},{28,24},{5,1},{9,5},{13... | collective-permute-start | bytes 1572872 | tf_op jit(solution)/shard_map/ppermute | solution.py:29
  109.1 25.9 %collective-permute-start.9 = (bf16[1024,256]{1,0:T(8,128)(2,1)S(1)}, bf16[1024,256]{1,0:T(8,128)(2,1)S(1)}, u32[]{:S(2)}, u32[]{:S(2)}) collective-permute-start(bf16[1024,256]{1,0:T(8,128)(2,1)S(1)} %get-tuple-element.3), channel_id=1, source_target_pairs={{0,4},{4,8},{8,12},{12,16},{16,20},{20,24},{24,28},{1,5},{5,9},{9,... | collective-permute-start | bytes 1572872 | tf_op jit(solution)/shard_map/ppermute | solution.py:27
  143.6 4.9 %collective-permute-start.11 = (bf16[16,256]{1,0:T(8,128)(2,1)S(1)}, bf16[16,256]{1,0:T(8,128)(2,1)S(1)}, u32[]{:S(2)}, u32[]{:S(2)}) collective-permute-start(bf16[16,256]{1,0:T(8,128)(2,1)S(1)} %gather_fusion.3), channel_id=1, source_target_pairs={{0,31},{1,0},{2,1},{3,2},{4,3},{5,4},{6,5},{7,6},{8,7},{9,8},{10,9... | collective-permute-start | bytes 24584 | tf_op jit(solution)/shard_map/ppermute | solution.py:12
  148.6 4.4 %collective-permute-start.12 = (bf16[32,256]{1,0:T(8,128)(2,1)S(1)}, bf16[32,256]{1,0:T(8,128)(2,1)S(1)}, u32[]{:S(2)}, u32[]{:S(2)}) collective-permute-start(bf16[32,256]{1,0:T(8,128)(2,1)S(1)} %pad_maximum_fusion.7), channel_id=1, source_target_pairs={{0,30},{1,31},{2,0},{3,1},{4,2},{5,3},{6,4},{7,5},{8,6},{9,7},{10,... | collective-permute-start | bytes 49160 | tf_op jit(solution)/shard_map/ppermute | solution.py:12
  152.9 3.7 %collective-permute-start.13 = (bf16[64,256]{1,0:T(8,128)(2,1)S(1)}, bf16[64,256]{1,0:T(8,128)(2,1)S(1)}, u32[]{:S(2)}, u32[]{:S(2)}) collective-permute-start(bf16[64,256]{1,0:T(8,128)(2,1)S(1)} %pad_maximum_fusion.5), channel_id=1, source_target_pairs={{0,28},{1,29},{2,30},{3,31},{4,0},{5,1},{6,2},{7,3},{8,4},{9,5},{1... | collective-permute-start | bytes 98312 | tf_op jit(solution)/shard_map/ppermute | solution.py:12
  156.6 3.6 %collective-permute-start.14 = (bf16[128,256]{1,0:T(8,128)(2,1)S(1)}, bf16[128,256]{1,0:T(8,128)(2,1)S(1)}, u32[]{:S(2)}, u32[]{:S(2)}) collective-permute-start(bf16[128,256]{1,0:T(8,128)(2,1)S(1)} %pad_maximum_fusion.3), channel_id=1, source_target_pairs={{0,24},{1,25},{2,26},{3,27},{4,28},{5,29},{6,30},{7,31},{8,0},{9,1... | collective-permute-start | bytes 196616 | tf_op jit(solution)/shard_map/ppermute | solution.py:12
  160.2 8.8 %collective-permute-start.15 = (bf16[256,256]{1,0:T(8,128)(2,1)S(1)}, bf16[256,256]{1,0:T(8,128)(2,1)S(1)}, u32[]{:S(2)}, u32[]{:S(2)}) collective-permute-start(bf16[256,256]{1,0:T(8,128)(2,1)S(1)} %get-tuple-element.9), channel_id=1, source_target_pairs={{0,16},{1,17},{2,18},{3,19},{4,20},{5,21},{6,22},{7,23},{8,24},{9,... | collective-permute-start | bytes 393224 | tf_op jit(solution)/shard_map/ppermute | solution.py:12
  180.6 15.4 %collective-permute-start.16 = (bf16[1024,256]{1,0:T(8,128)(2,1)S(1)}, bf16[1024,256]{1,0:T(8,128)(2,1)S(1)}, u32[]{:S(2)}, u32[]{:S(2)}) collective-permute-start(bf16[1024,256]{1,0:T(8,128)(2,1)S(1)} %get-tuple-element.5), channel_id=1, source_target_pairs={{4,0},{8,4},{12,8},{16,12},{20,16},{24,20},{28,24},{5,1},{9,5},{13... | collective-permute-start | bytes 1572872 | tf_op jit(solution)/shard_map/ppermute | solution.py:39
  182.5 25.9 %collective-permute-start.17 = (bf16[1024,256]{1,0:T(8,128)(2,1)S(1)}, bf16[1024,256]{1,0:T(8,128)(2,1)S(1)}, u32[]{:S(2)}, u32[]{:S(2)}) collective-permute-start(bf16[1024,256]{1,0:T(8,128)(2,1)S(1)} %get-tuple-element.6), channel_id=1, source_target_pairs={{0,4},{4,8},{8,12},{12,16},{16,20},{20,24},{24,28},{1,5},{5,9},{9,... | collective-permute-start | bytes 1572872 | tf_op jit(solution)/shard_map/ppermute | solution.py:39
